TPU v7x, 256 devices: a whole 4x4x8 slice. The times are simulated.
256 devices in a mesh: seq: 16 (over z, core), head: 16 (over x, y).
Axes of the slice: x: 4, y: 4, z: 8, core: 2. Of those that a mesh axis runs over, the one named last changes fastest.
Arguments:
- hidden_in: bfloat16 [4, 128, 2048], P(None, None, 'seq'), may hold values from -6 to 6
- attn_gain: float32 [2048], P('seq'), may hold values from 0.1 to 1.9
- attn_router: bfloat16 [2048, 8], P('seq'), may hold values from -0.125 to 0.125
- query_weight: bfloat16 [2048, 8, 2048], P('seq', None, 'head'), may hold values from -0.125 to 0.125
- kv_weight: bfloat16 [2048, 4096], P('seq', 'head'), may hold values from -0.125 to 0.125
- out_weight: bfloat16 [8, 2048, 2048], P(None, 'head', 'seq'), may hold values from -0.09375 to 0.09375
- mlp_gain: float32 [2048], replicated, may hold values from 0.1 to 1.9
- mlp_router: bfloat16 [2048, 8], replicated, may hold values from -0.125 to 0.125
- gate_weight: bfloat16 [2048, 45056], P(None, ('seq', 'head')), may hold values from -0.125 to 0.125
- up_weight: bfloat16 [2048, 45056], P(None, ('seq', 'head')), may hold values from -0.125 to 0.125
- down_weight: bfloat16 [45056, 2048], P(('seq', 'head')), may hold values from -0.3125 to 0.3125
- cache: bfloat16 [196608, 4096], P('seq', 'head'), as said below
- token_req: int32 [196608], P('seq'), may hold values from -1 to 127, as said below
- attn_route: int32 [4, 128, 2], replicated, may hold values from 0 to 7, all different within a row
- mlp_route: int32 [4, 128, 2], replicated, may hold values from 0 to 7, all different within a row; in each aligned block of 512 rows (0 to 511, 512 to 1023, ..., all dimensions but the last counted through in order) at most 192 rows name the same one
- owner: int32 [128], replicated, may hold values from 0 to 15, as said below
Outputs:
- hidden_out: bfloat16 [4, 128, 2048], P(None, 'head', 'seq')
- new_cache: bfloat16 [160, 4, 4096], P('seq', None, 'head')
Inputs may be any that keep to these rules, and one draw needn't show every extreme that they name: `token_req`: slots form pages of 128; the live slots of a page belong to one request; request r has lengths[r] live slots; four requests have exactly 32768, every other at least one and less than 512. At most 10 requests share an owner, and some owner has exactly 10. `cache`: rows of empty slots hold values too. `attn_route`: the 2 experts of a token differ. `mlp_route`: the 2 experts of a token differ; over all 4 x 128 tokens no expert is chosen more than 192 times, and one is chosen exactly 192 times.
All inputs are finite; a program needn't handle non-finite values.
Results may differ from a plain program's by a relative error of at most 0.019.
Values may be sent and summed in bfloat16 or wider, within the bound.
No kernel may reach another device: no remote copies, remote signals or barrier semaphores. Data moves between devices by JAX's collectives and lax.ppermute only.
A program may use at most 64 MiB of HBM per device.

v0:
```python
import math
import jax
import jax.numpy as jnp
from jax import lax
from jax.sharding import PartitionSpec as P

D = 2048
HD = 128
FF = 5632
PAGE = 128
OWN_MAX = 10
epsilon = 1e-06
masked_score = -1e30


def frequency(width):
    return jnp.power(jnp.float32(10000.0), -2.0 * jnp.arange(width // 2, dtype=jnp.float32) / width)


def rotate(values, angles):
    half_width = values.shape[-1] // 2
    cosine = jnp.cos(angles)
    sine_part = jnp.sin(angles)
    lower_half = values[..., :half_width]
    upper_half = values[..., half_width:]
    return jnp.concatenate(
        [
            lower_half * cosine - upper_half * sine_part,
            upper_half * cosine + lower_half * sine_part,
        ],
        axis=-1,
    )


def on_device(
    hidden_in,
    attn_gain,
    attn_router,
    query_weight,
    kv_weight,
    out_weight,
    mlp_gain,
    mlp_router,
    gate_weight,
    up_weight,
    down_weight,
    cache,
    token_req,
    attn_route,
    mlp_route,
    owner,
):
    highest = lax.Precision.HIGHEST
    step_count, req_count, local_width = hidden_in.shape
    head_count = lax.axis_size("head")
    seq_index = lax.axis_index("seq")
    head_index = lax.axis_index("head")
    experts = query_weight.shape[1]
    heads_dev = kv_weight.shape[1] // (2 * HD)
    top_count = attn_route.shape[2]
    tok_rows = step_count * req_count
    queries_all = step_count * top_count
    hidden_f = hidden_in.astype(jnp.float32)
    squares = jnp.sum(hidden_f * hidden_f, axis=2)
    scaled = (hidden_f * attn_gain).astype(jnp.bfloat16).reshape(tok_rows, local_width)
    query_part = jnp.dot(
        scaled,
        query_weight.reshape(local_width, experts * heads_dev * HD),
        preferred_element_type=jnp.float32,
    ).reshape(step_count, req_count, experts, heads_dev * HD)
    kv_part = jnp.dot(scaled, kv_weight, preferred_element_type=jnp.float32).reshape(
        step_count, req_count, heads_dev * 2 * HD
    )
    logit_part = jnp.dot(scaled, attn_router, preferred_element_type=jnp.float32).reshape(
        step_count, req_count, experts
    )
    request_ids = jnp.arange(req_count, dtype=jnp.int32)
    counts = jnp.sum((token_req[:, None] == request_ids[None, :]).astype(jnp.float32), axis=0)
    attn_hot = (attn_route[..., None] == jnp.arange(experts, dtype=jnp.int32)).astype(jnp.float32)
    query_sum, kv_sum, logit_sum, square_sum, lengths = lax.psum(
        (query_part, kv_part, logit_part, squares, counts), "seq"
    )
    picked = jnp.einsum("srke,srec->srkc", attn_hot, query_sum, precision=highest)
    inverse = lax.rsqrt(square_sum / D + epsilon)
    attn_gates = jax.nn.softmax(
        jnp.sum(attn_hot * (logit_sum * inverse[..., None])[:, :, None, :], axis=3), axis=2
    )
    positions = lengths[None, :] + jnp.arange(step_count, dtype=jnp.float32)[:, None]
    freq_table = frequency(HD)
    queries = (picked * inverse[..., None, None]).reshape(
        step_count, req_count, top_count, heads_dev, HD
    )
    queries = rotate(queries, positions[:, :, None, None, None] * freq_table).astype(jnp.bfloat16)
    projected = kv_sum.reshape(step_count, req_count, heads_dev, 2 * HD) * inverse[..., None, None]
    new_keys = rotate(projected[..., :HD], positions[:, :, None, None] * freq_table).astype(
        jnp.bfloat16
    )
    new_values = projected[..., HD:].astype(jnp.bfloat16)
    new_rows = jnp.concatenate([new_keys, new_values], axis=3).reshape(
        step_count, req_count, heads_dev * 2 * HD
    )
    owned_flag = (owner == seq_index).astype(jnp.int32)
    before = (request_ids[None, :] < request_ids[:, None]).astype(jnp.int32)
    slot_rank = jnp.sum(before * owned_flag[None, :], axis=1)
    slot_ids = jnp.arange(OWN_MAX, dtype=jnp.int32)
    select = ((owned_flag[None, :] == 1) & (slot_rank[None, :] == slot_ids[:, None])).astype(
        jnp.bfloat16
    )
    appended = jnp.einsum(
        "jr,src->jsc", select, new_rows, preferred_element_type=jnp.float32
    ).astype(jnp.bfloat16)
    page_total = token_req.shape[0] // PAGE
    page_owner = token_req.reshape(page_total, PAGE)
    page_req = jnp.max(page_owner, axis=1)
    page_pick = jnp.maximum(page_req, 0)
    live_slot = page_owner >= 0
    req_hot = (page_req[None, :] == request_ids[:, None]).astype(jnp.float32)
    query_rows = jnp.transpose(queries, (1, 3, 0, 2, 4)).reshape(
        req_count, heads_dev, queries_all, HD
    )
    page_queries = query_rows[page_pick]
    paged = cache.reshape(page_total, PAGE, heads_dev, 2 * HD)
    score_scale = 1.0 / math.sqrt(HD)
    scores = (
        jnp.einsum(
            "phqd,pthd->phqt", page_queries, paged[..., :HD], preferred_element_type=jnp.float32
        )
        * score_scale
    )
    scores = jnp.where(live_slot[:, None, None, :], scores, masked_score)
    fresh_keys = jnp.transpose(new_keys, (1, 2, 0, 3))
    fresh_values = jnp.transpose(new_values, (1, 2, 0, 3))
    fresh_scores = (
        jnp.einsum("rhqd,rhsd->rhqs", query_rows, fresh_keys, preferred_element_type=jnp.float32)
        * score_scale
    )
    query_step = jnp.arange(queries_all) // top_count
    causal = jnp.arange(step_count)[None, :] <= query_step[:, None]
    fresh_live = causal[None, None, :, :] & (owned_flag[:, None, None, None] == 1)
    fresh_scores = jnp.where(fresh_live, fresh_scores, masked_score)
    page_best = jnp.max(scores, axis=3)
    local_best = jnp.max(
        jnp.where(req_hot[:, :, None, None] > 0, page_best[None], masked_score), axis=1
    )
    local_best = jnp.maximum(local_best, jnp.max(fresh_scores, axis=3))
    maxima = lax.pmax(local_best, "seq")
    page_probs = jnp.where(
        live_slot[:, None, None, :], jnp.exp(scores - maxima[page_pick][..., None]), 0.0
    )
    page_sums = jnp.sum(page_probs, axis=3)
    page_out = jnp.einsum(
        "phqt,pthd->phqd",
        page_probs.astype(jnp.bfloat16),
        paged[..., HD:],
        preferred_element_type=jnp.float32,
    )
    fresh_probs = jnp.where(fresh_live, jnp.exp(fresh_scores - maxima[..., None]), 0.0)
    totals = jnp.einsum("rp,phq->rhq", req_hot, page_sums, precision=highest) + jnp.sum(
        fresh_probs, axis=3
    )
    outputs = jnp.einsum("rp,phqd->rhqd", req_hot, page_out, precision=highest)
    outputs = outputs + jnp.einsum(
        "rhqs,rhsd->rhqd",
        fresh_probs.astype(jnp.bfloat16),
        fresh_values,
        preferred_element_type=jnp.float32,
    )
    local_totals = totals
    local_outputs = outputs
    totals, outputs = (
        lax.psum(local_totals.astype(jnp.bfloat16), "seq").astype(jnp.float32),
        lax.psum(local_outputs.astype(jnp.bfloat16), "seq").astype(jnp.float32),
    )
    attention = outputs / totals[..., None]
    attention = jnp.transpose(
        attention.reshape(req_count, heads_dev, step_count, top_count, HD), (2, 0, 3, 1, 4)
    )
    weighted = (attention * attn_gates[..., None, None]).astype(jnp.bfloat16)
    mixed = jnp.einsum(
        "srkhd,srke->srehd", weighted.astype(jnp.float32), attn_hot, precision=highest
    ).astype(jnp.bfloat16)
    head_part = jnp.dot(
        mixed.reshape(tok_rows, experts * heads_dev * HD),
        out_weight.reshape(experts * heads_dev * HD, local_width),
        preferred_element_type=jnp.float32,
    ).reshape(step_count, req_count, local_width)
    attn_out = lax.psum(head_part.astype(jnp.bfloat16), "head").astype(jnp.float32)
    residual = (hidden_f + attn_out).astype(jnp.bfloat16)
    full_rows = lax.all_gather(residual, "seq", axis=2, tiled=True)
    full_f = full_rows.astype(jnp.float32)
    inverse_mlp = lax.rsqrt(jnp.mean(full_f * full_f, axis=2) + epsilon)
    normed = (full_f * inverse_mlp[..., None] * mlp_gain).astype(jnp.bfloat16).reshape(tok_rows, D)
    mlp_logits = jnp.dot(normed, mlp_router, preferred_element_type=jnp.float32).reshape(
        step_count, req_count, experts
    )
    mlp_hot = (mlp_route[..., None] == jnp.arange(experts, dtype=jnp.int32)).astype(jnp.float32)
    mlp_gates = jax.nn.softmax(jnp.sum(mlp_hot * mlp_logits[:, :, None, :], axis=3), axis=2)
    combine_w = jnp.sum(mlp_hot * mlp_gates[..., None], axis=2)
    unit_count = gate_weight.shape[1]
    device_index = seq_index * head_count + head_index
    expert_index = device_index * unit_count // FF
    expert_ids = jnp.arange(experts, dtype=jnp.int32)
    rows_dev = req_count // head_count
    expert_weight = jnp.sum(
        combine_w * (expert_ids == expert_index).astype(jnp.float32), axis=2
    ).reshape(tok_rows, 1)
    gate_pre = jnp.dot(normed, gate_weight, preferred_element_type=jnp.float32)
    up_pre = jnp.dot(normed, up_weight, preferred_element_type=jnp.float32)
    hidden_units = (jax.nn.silu(gate_pre) * up_pre).astype(jnp.bfloat16)
    expert_term = (
        jnp.dot(hidden_units, down_weight, preferred_element_type=jnp.float32) * expert_weight
    ).reshape(step_count, req_count, D)
    by_columns = lax.psum_scatter(
        expert_term.astype(jnp.bfloat16), "seq", scatter_dimension=2, tiled=True
    )
    expert_part = lax.psum_scatter(by_columns, "head", scatter_dimension=1, tiled=True).astype(
        jnp.float32
    )
    own_rows = lax.dynamic_slice_in_dim(residual, head_index * rows_dev, rows_dev, 1)
    hidden_out = (own_rows.astype(jnp.float32) + expert_part).astype(jnp.bfloat16)
    return (hidden_out, appended)


def solution(mesh):
    in_specs = (
        P(None, None, "seq"),
        P("seq"),
        P("seq", None),
        P("seq", None, "head"),
        P("seq", "head"),
        P(None, "head", "seq"),
        P(),
        P(),
        P(None, ("seq", "head")),
        P(None, ("seq", "head")),
        P(("seq", "head"), None),
        P("seq", "head"),
        P("seq"),
        P(),
        P(),
        P(),
    )
    out_specs = (P(None, "head", "seq"), P("seq", None, "head"))
    return jax.shard_map(
        on_device, mesh=mesh, in_specs=in_specs, out_specs=out_specs, check_vma=False
    )
```

profile of v0, /device:TPU:2, one launch (start us, length us, event | category | flops | bytes accessed | tf_op | source)
XLA Modules:
  0.0 634.6 jit_solution(8452154288114500692)
XLA Ops:
  7.2 1.1 copy.167
  8.5 2.0 fusion.79
  10.4 2.7 fusion.67
  13.4 5.5 convert_reduce_fusion
  19.2 50.9 %all-reduce.1 = (f32[4,128]{1,0:T(4,128)S(1)}, f32[128]{0:T(128)S(1)}, f32[4,128,8]{1,2,0:T(8,128)S(1)}) all-reduce(f32[4,128]{1,0:T(4,128)S(1)} %fusion.46, f32[128]{0:T(128)S(1)} %convert_reduce_fusion, f32[4,128,8]{1,2,0:T(8,128)S(1)} %fusion.77), channel_id=1, replica_groups=mesh['seq'=16,'head'=16] {'seq'}, use_global_device_ids=true, to_apply=%region_3.0 | all-reduce | flops 4736 | bytes 37888 | tf_op jit(solution)/shard_map/psum | solution.py:80
  70.6 7.3 %select_reduce_fusion.2 = f32[4,128,2]{2,1,0:T(8,128)S(1)} fusion(f32[4,128,8]{2,1,0:T(8,128)S(1)} %copy.124, s32[4,128,2]{2,1,0:T(8,128)S(1)} %copy.111), kind=kLoop, calls=%fused_computation.46 | loop fusion | flops 23552 | bytes 24576 | tf_op jit(solution)/shard_map/reduce_sum | solution.py:86
  77.8 0.8 fusion.103
  78.8 1.0 multiply_cosine_fusion.1
  79.8 53.4 %all-reduce.14.cloned.1.call-done = (f32[4,128,256]{2,1,0:T(8,128)}, f32[4,128,8,128]{3,1,2,0:T(8,128)}) async-done(((f32[4,128,256]{2,1,0:T(8,128)}, f32[4,128,8,128]{3,1,2,0:T(8,128)}), (f32[4,128,256]{2,1,0:T(8,128)}, f32[4,128,8,128]{3,1,2,0:T(8,128)})) %all-reduce.14.cloned.1.call-update) | async-done | bytes 2621456 | tf_op jit(solution)/shard_map/psum | solution.py:80
  133.2 1.3 multiply_bitcast_fusion
  134.5 1.2 fusion.42
  135.8 3.2 fusion.12
  138.9 0.8 subtract_convert_fusion
  139.8 0.7 maximum_bitcast_fusion
  140.7 0.7 gather_fusion
  141.4 3.7 fusion.101
  145.5 0.5 fusion.102
  146.0 48.3 %pmax.7 = f32[128,1,8]{2,0,1:T(8,128)S(1)} all-reduce(f32[128,1,8]{2,0,1:T(8,128)S(1)} %maximum_bitcast_fusion.4), channel_id=1, replica_groups=mesh['seq'=16,'head'=16] {'seq'}, use_global_device_ids=true, to_apply=%region_10.0 | all-reduce | flops 1024 | bytes 8192 | tf_op jit(solution)/shard_map/pmax | solution.py:146
  194.3 0.6 gather_fusion.1
  194.9 2.9 fusion.5
  198.4 0.7 fusion.65
  199.1 1.3 fusion.21
  200.7 23.6 %psum.61 = bf16[128,8]{0,1:T(8,128)(2,1)S(1)} all-reduce(bf16[128,8]{0,1:T(8,128)(2,1)S(1)} %fusion.26), channel_id=1, replica_groups=mesh['seq'=16,'head'=16] {'seq'}, use_global_device_ids=true, to_apply=%region_14.15 | all-reduce | flops 1024 | bytes 4096 | tf_op jit(solution)/shard_map/psum | solution.py:171
  224.3 83.3 %all-reduce.8.cloned.1.call-done = bf16[128,1,8,128]{3,0,2,1:T(8,128)(2,1)} async-done(((bf16[128,1,8,128]{3,0,2,1:T(8,128)(2,1)}), bf16[128,1,8,128]{3,0,2,1:T(8,128)(2,1)}) %all-reduce.8.cloned.1.call-update) | async-done | bytes 262160 | tf_op jit(solution)/shard_map/psum | solution.py:172
  307.6 1.2 convert_divide_fusion
  308.8 2.7 convolution_convert_fusion
  311.6 1.1 fusion.25
  312.7 92.5 %all-reduce.10.cloned.1.call-done = bf16[4,128,128]{2,1,0:T(8,128)(2,1)} async-done(((bf16[4,128,128]{2,1,0:T(8,128)(2,1)}), bf16[4,128,128]{2,1,0:T(8,128)(2,1)}) %all-reduce.10.cloned.1.call-update) | async-done | bytes 131088 | tf_op jit(solution)/shard_map/psum | solution.py:187
  405.2 1.6 fusion.47
  407.1 40.6 %all-gather.2.cloned.1.call-done = bf16[4,128,2048]{2,1,0:T(8,128)(2,1)} async-done(((bf16[4,128,128]{2,1,0:T(8,128)(2,1)}), bf16[4,128,2048]{2,1,0:T(8,128)(2,1)}) %all-gather.2.cloned.1.call-update) | async-done | bytes 2097168 | tf_op jit(solution)/shard_map/all_gather | solution.py:189
  447.7 2.2 fusion.2
  450.0 0.5 fusion.4
  450.5 1.3 copy-done.2
  451.9 0.7 fusion.85
  452.6 7.3 %select_reduce_fusion.1 = f32[4,128,2]{2,1,0:T(8,128)S(1)} fusion(f32[4,128,8]{2,1,0:T(8,128)S(1)} %fusion.85, s32[4,128,2]{2,1,0:T(8,128)S(1)} %copy.126), kind=kLoop, calls=%fused_computation.44 | loop fusion | flops 23552 | bytes 24576 | tf_op jit(solution)/shard_map/reduce_sum | solution.py:197
  460.1 1.4 select_reduce_fusion
  461.7 3.5 fusion.104
  465.2 4.1 multiply_convert_fusion
  469.4 3.1 copy.133
  472.5 1.7 copy.166
  474.3 0.6 copy-done.17
  474.9 0.6 dynamic-slice
  476.2 56.6 %reduce-scatter.5.cloned.1.call-done = bf16[128,512]{1,0:T(8,128)(2,1)} async-done(((bf16[2048,512]{1,0:T(8,128)(2,1)}), bf16[128,512]{1,0:T(8,128)(2,1)}) %reduce-scatter.5.cloned.1.call-update) | async-done | bytes 131088
  532.9 0.9 reshape.447
  533.8 0.8 copy.134
  534.9 0.6 copy.129
  535.5 91.0 %all-reduce.12.cloned.1.call-done = bf16[4,128,128]{2,1,0:T(8,128)(2,1)} async-done(((bf16[4,128,128]{2,1,0:T(8,128)(2,1)}), bf16[4,128,128]{2,1,0:T(8,128)(2,1)}) %all-reduce.12.cloned.1.call-update) | async-done | bytes 131088
  626.5 1.3 add_convert_fusion.1
  (84 shorter events, 4.1 us)
Async XLA Ops:
  7.2 458.1 %copy-start = (bf16[176,2048]{1,0:T(8,128)(2,1)S(1)}, bf16[176,2048]{1,0:T(8,128)(2,1)}, u32[]{:S(2)}) copy-start(bf16[176,2048]{1,0:T(8,128)(2,1)} %param.26) | copy-start | bytes 2162692
  7.2 126.0 %all-reduce.14.cloned.1.call-start = ((), (), s32[]{:S(2)}) async-start(), calls=%async_computation.6 | async-start | bytes 5242880 | tf_op jit(solution)/shard_map/psum | solution.py:80
  10.4 2.8 copy-start.4
  10.4 3.0 copy-start.7
  10.4 8.7 %copy-start.11 = (f32[128]{0:T(128)S(1)}, f32[128]{0:T(128)}, u32[]{:S(2)}) copy-start(f32[128]{0:T(128)} %param.17) | copy-start | bytes 1540
  10.4 8.7 %copy-start.16 = (bf16[128,8]{0,1:T(8,128)(2,1)S(1)}, bf16[128,8]{0,1:T(8,128)(2,1)}, u32[]{:S(2)}) copy-start(bf16[128,8]{0,1:T(8,128)(2,1)} %param.18) | copy-start | bytes 6148
  13.1 57.1 %copy-start.12 = (s32[128]{0:T(128)S(1)}, s32[128]{0:T(128)}, u32[]{:S(2)}) copy-start(s32[128]{0:T(128)} %param.31) | copy-start | bytes 1540
  13.1 57.1 %copy-start.9 = (s32[4,128,2]{1,2,0:T(2,128)S(1)}, s32[4,128,2]{1,2,0:T(2,128)}, u32[]{:S(2)}) copy-start(s32[4,128,2]{1,2,0:T(2,128)} %param.29) | copy-start | bytes 12292
  13.2 294.5 %all-reduce.8.cloned.1.call-start = ((), (), s32[]{:S(2)}) async-start(), calls=%async_computation.1 | async-start | bytes 524288 | tf_op jit(solution)/shard_map/psum | solution.py:172
  133.2 2.6 copy-start.13
  135.7 9.7 %copy-start.5 = (bf16[4,128,1,64]{3,1,0,2:T(8,128)(2,1)}, bf16[4,128,1,64]{3,1,0,2:T(8,128)(2,1)S(1)}, u32[]{:S(2)}) copy-start(bf16[4,128,1,64]{3,1,0,2:T(8,128)(2,1)S(1)} %get-tuple-element.26) | copy-start | bytes 196612
  200.4 204.9 %all-reduce.10.cloned.1.call-start = ((), (), s32[]{:S(2)}) async-start(), calls=%async_computation.2 | async-start | bytes 262144 | tf_op jit(solution)/shard_map/psum | solution.py:187
  308.8 2.7 copy-start.14
  311.5 95.4 %copy-start.10 = (s32[4,128,2]{1,2,0:T(2,128)S(1)}, s32[4,128,2]{1,2,0:T(2,128)}, u32[]{:S(2)}) copy-start(s32[4,128,2]{1,2,0:T(2,128)} %param.30) | copy-start | bytes 12292
  311.6 138.4 %copy-start.8 = (f32[2048]{0:T(1024)S(1)}, f32[2048]{0:T(1024)}, u32[]{:S(2)}) copy-start(f32[2048]{0:T(1024)} %param.22) | copy-start | bytes 24580
  312.7 135.0 %all-gather.2.cloned.1.call-start = ((), (), s32[]{:S(2)}) async-start(), calls=%async_computation.3 | async-start | bytes 2228224 | tf_op jit(solution)/shard_map/all_gather | solution.py:189
  406.8 126.0 %reduce-scatter.5.cloned.1.call-start = ((), (), s32[]{:S(2)}) async-start(), calls=%async_computation.4 | async-start | bytes 2228224
  447.7 2.2 copy-start.1
  450.0 1.9 copy-start.15
  450.5 1.4 copy-start.2
  461.7 3.5 copy-start.3
  474.2 0.7 copy-start.17
  474.2 60.4 %copy-start.6 = (bf16[4,128,1,64]{3,1,0,2:T(8,128)(2,1)S(1)}, bf16[4,128,1,64]{3,1,0,2:T(8,128)(2,1)}, u32[]{:S(2)}) copy-start(bf16[4,128,1,64]{3,1,0,2:T(8,128)(2,1)} %copy-done.5) | copy-start | bytes 196612
  474.2 152.2 %all-reduce.12.cloned.1.call-start = ((), (), s32[]{:S(2)}) async-start(), calls=%async_computation.5 | async-start | bytes 262144
Sparse Core Ops, SparseCore 0:
  13.3 119.8 all-reduce.13
  200.5 107.0 all-reduce.7
  312.8 92.3 all-reduce.9
  407.0 40.6 all-gather.1
  474.3 58.4 reduce-scatter.4
  535.9 90.5 all-reduce.11
where the time goes:
time: 635 us
  waiting for transfers between devices  418 us (66%)
  blocking collectives  123 us (19%)
  other arithmetic  36 us (6%)
  matrix products  29.6 us (5%)
  between operations  15.3 us (2%)
  local copies, waits for them, and re-layouts  13.2 us (2%)
    unnamed x8, waiting for transfers between devices  148 us
    psum x1, waiting for transfers between devices, on_device(): lax.psum(head_part.astype(jnp.bfloat16), 'head').astype(jnp.float32)  92.5 us
    psum x1, waiting for transfers between devices, on_device(): lax.psum(local_outputs.astype(jnp.bfloat16), 'seq').astype(jnp.float32)  83.3 us
    psum x1, waiting for transfers between devices, on_device(): lax.psum((query_part, kv_part, logit_part, squares, counts), 'seq')  53.4 us
    psum x1, blocking collectives, on_device(): lax.psum((query_part, kv_part, logit_part, squares, counts), 'seq')  50.9 us
    pmax x1, blocking collectives, on_device(): maxima = lax.pmax(local_best, 'seq')  48.3 us
    all_gather x1, waiting for transfers between devices, on_device(): full_rows = lax.all_gather(residual, 'seq', axis=2, tiled=True)  40.6 us
    psum x1, blocking collectives, on_device(): lax.psum(local_totals.astype(jnp.bfloat16), 'seq').astype(jnp.float32)  23.6 us
  transfers between devices with their start and end apart: 6, of which 6 were waited for; matrix products, arithmetic and copies ran while one was open for 3% of the time, Pallas kernels for 0%

commit v1 on v0

--- a/solution.py
+++ b/solution.py
@@ -11,6 +11,12 @@
 OWN_MAX = 10
 epsilon = 1e-06
 masked_score = -1e30
+
+
+def joined_along(parts, dim):
+    parts = jnp.moveaxis(parts, 0, dim)
+    shape = parts.shape
+    return parts.reshape(*shape[:dim], shape[dim] * shape[dim + 1], *shape[dim + 2 :])
 
 
 def frequency(width):
@@ -186,7 +192,19 @@
     ).reshape(step_count, req_count, local_width)
     attn_out = lax.psum(head_part.astype(jnp.bfloat16), "head").astype(jnp.float32)
     residual = (hidden_f + attn_out).astype(jnp.bfloat16)
-    full_rows = lax.all_gather(residual, "seq", axis=2, tiled=True)
+    size = lax.axis_size("seq")
+    pairs = [(i, (i + 1) % size) for i in range(size)]
+    back = [(b, a) for a, b in pairs]
+    lower, upper = ([], [])
+    for step in range(size - 1):
+        if step % 2 == 0:
+            lower.append(lax.ppermute(lower[-1] if lower else residual, "seq", pairs))
+        else:
+            upper.append(lax.ppermute(upper[-1] if upper else residual, "seq", back))
+    blocks = jnp.stack([*lower[::-1], residual, *upper])
+    shift = lax.axis_index("seq") - len(lower)
+    blocks = blocks[(jnp.arange(size) - shift) % size]
+    full_rows = joined_along(blocks, 2)
     full_f = full_rows.astype(jnp.float32)
     inverse_mlp = lax.rsqrt(jnp.mean(full_f * full_f, axis=2) + epsilon)
     normed = (full_f * inverse_mlp[..., None] * mlp_gain).astype(jnp.bfloat16).reshape(tok_rows, D)

time: 635 us -> 666 us (1.049)
  local copies, waits for them, and re-layouts: 13.2 us -> 38.1 us
  starting transfers between devices: 0.25 us -> 20.9 us
  waiting for transfers between devices: 418 us -> 401 us
    all_gather x1 -> x0, waiting for transfers between devices: 40.6 us -> none  [on_device(): full_rows = lax.all_gather(residual, 'seq', axis=2, tiled=True)]
    ppermute x0 -> x15, waiting for transfers between devices: none -> 23.2 us  [the longest x8 23.2 us: on_device(): lower.append(lax.ppermute(lower[-1] if lower else residual, 'seq', pairs))]
    ppermute x0 -> x15, starting transfers between devices: none -> 20.7 us  [the longest x7 20.7 us: on_device(): upper.append(lax.ppermute(upper[-1] if upper else residual, 'seq', back))]
    convert_element_type x0 -> x2, local copies, waits for them, and re-layouts: none -> 12.1 us  [on_device(): full_f = full_rows.astype(jnp.float32)]
    unnamed x45 -> x64, local copies, waits for them, and re-layouts: 11.1 us -> 20.8 us
    unnamed x8 -> x7, waiting for transfers between devices: 148 us -> 148 us
  transfers between devices with their start and end apart: 6 -> 20, of which waited for: 6 -> 13; matrix products, arithmetic and copies ran while one was open for 3% -> 4% of each run, Pallas kernels for 0% -> 0%
where the time goes in v1:
time: 666 us; the launch traced here: 665 us
  waiting for transfers between devices  401 us (60%)
  blocking collectives  123 us (18%)
  other arithmetic  40.2 us (6%)
  local copies, waits for them, and re-layouts  38.1 us (6%)
  matrix products  27.7 us (4%)
  starting transfers between devices  20.9 us (3%)
  between operations  14.9 us (2%)
    unnamed x7, waiting for transfers between devices  148 us
    psum x1, waiting for transfers between devices, on_device(): lax.psum(head_part.astype(jnp.bfloat16), 'head').astype(jnp.float32)  92.5 us
    psum x1, waiting for transfers between devices, on_device(): lax.psum(local_outputs.astype(jnp.bfloat16), 'seq').astype(jnp.float32)  83.4 us
    psum x1, waiting for transfers between devices, on_device(): lax.psum((query_part, kv_part, logit_part, squares, counts), 'seq')  53.4 us
    psum x1, blocking collectives, on_device(): lax.psum((query_part, kv_part, logit_part, squares, counts), 'seq')  50.9 us
    pmax x1, blocking collectives, on_device(): maxima = lax.pmax(local_best, 'seq')  48.3 us
    psum x1, blocking collectives, on_device(): lax.psum(local_totals.astype(jnp.bfloat16), 'seq').astype(jnp.float32)  23.6 us
    ppermute x8, waiting for transfers between devices, on_device(): lower.append(lax.ppermute(lower[-1] if lower else residual, 'seq', pairs))  23.2 us
  transfers between devices with their start and end apart: 20, of which 13 were waited for; matrix products, arithmetic and copies ran while one was open for 4% of the time, Pallas kernels for 0%

profile of v1, /device:TPU:2, one launch (start us, length us, event | category | flops | bytes accessed | tf_op | source)
XLA Modules:
  0.0 665.4 jit_solution(17527002563581688016)
XLA Ops:
  8.5 2.0 fusion.81
  10.4 2.7 fusion.69
  13.3 5.5 convert_reduce_fusion
  19.3 50.9 %all-reduce.1 = (f32[4,128]{1,0:T(4,128)S(1)}, f32[128]{0:T(128)S(1)}, f32[4,128,8]{1,2,0:T(8,128)S(1)}) all-reduce(f32[4,128]{1,0:T(4,128)S(1)} %fusion.48, f32[128]{0:T(128)S(1)} %convert_reduce_fusion, f32[4,128,8]{1,2,0:T(8,128)S(1)} %fusion.79), channel_id=1, replica_groups=mesh['seq'=16,'head'=16] {'seq'}, use_global_device_ids=true, to_apply=%region_3.0 | all-reduce | flops 4736 | bytes 37888 | tf_op jit(solution)/shard_map/psum | solution.py:86
  70.5 7.3 %select_reduce_fusion.2 = f32[4,128,2]{2,1,0:T(8,128)S(1)} fusion(f32[4,128,8]{2,1,0:T(8,128)S(1)} %copy.139, s32[4,128,2]{2,1,0:T(8,128)S(1)} %copy.126), kind=kLoop, calls=%fused_computation.51 | loop fusion | flops 23552 | bytes 24576 | tf_op jit(solution)/shard_map/reduce_sum | solution.py:92
  79.7 53.4 %all-reduce.14.cloned.1.call-done = (f32[4,128,256]{2,1,0:T(8,128)}, f32[4,128,8,128]{3,1,2,0:T(8,128)}) async-done(((f32[4,128,256]{2,1,0:T(8,128)}, f32[4,128,8,128]{3,1,2,0:T(8,128)}), (f32[4,128,256]{2,1,0:T(8,128)}, f32[4,128,8,128]{3,1,2,0:T(8,128)})) %all-reduce.14.cloned.1.call-update) | async-done | bytes 2621456 | tf_op jit(solution)/shard_map/psum | solution.py:86
  133.2 1.3 multiply_bitcast_fusion
  134.5 1.2 fusion.44
  135.8 3.2 fusion.14
  141.4 3.7 fusion.106
  146.0 48.3 %pmax.7 = f32[128,1,8]{2,0,1:T(8,128)S(1)} all-reduce(f32[128,1,8]{2,0,1:T(8,128)S(1)} %maximum_bitcast_fusion.4), channel_id=1, replica_groups=mesh['seq'=16,'head'=16] {'seq'}, use_global_device_ids=true, to_apply=%region_10.0 | all-reduce | flops 1024 | bytes 8192 | tf_op jit(solution)/shard_map/pmax | solution.py:152
  195.2 2.9 fusion.7
  199.1 1.3 fusion.23
  200.7 23.6 %psum.61 = bf16[128,8]{0,1:T(8,128)(2,1)S(1)} all-reduce(bf16[128,8]{0,1:T(8,128)(2,1)S(1)} %fusion.28), channel_id=1, replica_groups=mesh['seq'=16,'head'=16] {'seq'}, use_global_device_ids=true, to_apply=%region_14.15 | all-reduce | flops 1024 | bytes 4096 | tf_op jit(solution)/shard_map/psum | solution.py:177
  224.3 83.4 %all-reduce.8.cloned.1.call-done = bf16[128,1,8,128]{3,0,2,1:T(8,128)(2,1)} async-done(((bf16[128,1,8,128]{3,0,2,1:T(8,128)(2,1)}), bf16[128,1,8,128]{3,0,2,1:T(8,128)(2,1)}) %all-reduce.8.cloned.1.call-update) | async-done | bytes 262160 | tf_op jit(solution)/shard_map/psum | solution.py:178
  307.6 1.2 convert_divide_fusion
  308.8 2.7 convolution_convert_fusion
  311.6 1.1 fusion.27
  312.7 92.5 %all-reduce.10.cloned.1.call-done = bf16[4,128,128]{2,1,0:T(8,128)(2,1)} async-done(((bf16[4,128,128]{2,1,0:T(8,128)(2,1)}), bf16[4,128,128]{2,1,0:T(8,128)(2,1)}) %all-reduce.10.cloned.1.call-update) | async-done | bytes 131088 | tf_op jit(solution)/shard_map/psum | solution.py:193
  406.2 5.6 collective-permute-done
  411.8 3.0 collective-permute-start.8
  414.8 2.6 collective-permute-done.1
  417.4 3.0 collective-permute-start.9
  420.4 2.6 collective-permute-done.2
  423.0 3.0 collective-permute-start.10
  426.0 2.6 collective-permute-done.3
  428.6 3.0 collective-permute-start.11
  431.6 2.6 collective-permute-done.4
  434.3 3.0 collective-permute-start.12
  437.2 2.6 collective-permute-done.5
  439.9 3.0 collective-permute-start.13
  442.8 2.6 collective-permute-done.6
  446.4 3.0 collective-permute-start.14
  449.3 1.7 collective-permute-done.7
  461.6 2.5 gather_fusion.2
  464.6 2.5 convert_bitcast_fusion
  467.1 5.4 copy.143
  472.5 6.7 %copy.141 = f32[4,128,16,128]{3,2,1,0:T(8,128)} copy(f32[4,128,16,128]{3,1,0,2:T(8,128)} %convert_bitcast_fusion) | data formatting | bytes 8388608 | tf_op jit(solution)/shard_map/convert_element_type | solution.py:208
  480.9 7.3 %select_reduce_fusion.1 = f32[4,128,2]{2,1,0:T(8,128)S(1)} fusion(f32[4,128,8]{2,1,0:T(8,128)S(1)} %fusion.87, s32[4,128,2]{2,1,0:T(8,128)S(1)} %copy-done.2), kind=kLoop, calls=%fused_computation.49 | loop fusion | flops 23552 | bytes 24576 | tf_op jit(solution)/shard_map/reduce_sum | solution.py:215
  488.4 1.4 select_reduce_fusion
  490.0 4.1 fusion.4
  494.1 1.6 fusion.109
  495.8 4.2 multiply_convert_fusion
  499.9 3.1 copy.152
  503.0 1.7 copy.187
  506.8 57.2 %reduce-scatter.5.cloned.1.call-done = bf16[128,512]{1,0:T(8,128)(2,1)} async-done(((bf16[2048,512]{1,0:T(8,128)(2,1)}), bf16[128,512]{1,0:T(8,128)(2,1)}) %reduce-scatter.5.cloned.1.call-update) | async-done | bytes 131088
  566.6 90.9 %all-reduce.12.cloned.1.call-done = bf16[4,128,128]{2,1,0:T(8,128)(2,1)} async-done(((bf16[4,128,128]{2,1,0:T(8,128)(2,1)}), bf16[4,128,128]{2,1,0:T(8,128)(2,1)}) %all-reduce.12.cloned.1.call-update) | async-done | bytes 131088
  657.6 1.3 add_convert_fusion.1
  (138 shorter events, 28.7 us)
Async XLA Ops:
  7.2 488.6 %copy-start = (bf16[176,2048]{1,0:T(8,128)(2,1)S(1)}, bf16[176,2048]{1,0:T(8,128)(2,1)}, u32[]{:S(2)}) copy-start(bf16[176,2048]{1,0:T(8,128)(2,1)} %param.26) | copy-start | bytes 2162692
  7.2 126.0 %all-reduce.14.cloned.1.call-start = ((), (), s32[]{:S(2)}) async-start(), calls=%async_computation.5 | async-start | bytes 5242880 | tf_op jit(solution)/shard_map/psum | solution.py:86
  10.4 2.8 copy-start.8
  10.4 8.4 %copy-start.3 = (bf16[4,128,128]{2,1,0:T(8,128)(2,1)S(1)}, bf16[4,128,128]{2,1,0:T(8,128)(2,1)}, u32[]{:S(2)}) copy-start(bf16[4,128,128]{2,1,0:T(8,128)(2,1)} %param.16) | copy-start | bytes 393220
  10.4 8.7 %copy-start.12 = (f32[128]{0:T(128)S(1)}, f32[128]{0:T(128)}, u32[]{:S(2)}) copy-start(f32[128]{0:T(128)} %param.17) | copy-start | bytes 1540
  10.4 8.7 %copy-start.18 = (bf16[128,8]{0,1:T(8,128)(2,1)S(1)}, bf16[128,8]{0,1:T(8,128)(2,1)}, u32[]{:S(2)}) copy-start(bf16[128,8]{0,1:T(8,128)(2,1)} %param.18) | copy-start | bytes 6148
  13.1 6.1 copy-start.13
  13.1 57.2 %copy-start.10 = (s32[4,128,2]{1,2,0:T(2,128)S(1)}, s32[4,128,2]{1,2,0:T(2,128)}, u32[]{:S(2)}) copy-start(s32[4,128,2]{1,2,0:T(2,128)} %param.29) | copy-start | bytes 12292
  13.2 294.5 %all-reduce.8.cloned.1.call-start = ((), (), s32[]{:S(2)}) async-start(), calls=%async_computation.1 | async-start | bytes 524288 | tf_op jit(solution)/shard_map/psum | solution.py:178
  133.2 2.6 copy-start.14
  135.7 9.6 %copy-start.4 = (bf16[4,128,1,64]{3,1,0,2:T(8,128)(2,1)}, bf16[4,128,1,64]{3,1,0,2:T(8,128)(2,1)S(1)}, u32[]{:S(2)}) copy-start(bf16[4,128,1,64]{3,1,0,2:T(8,128)(2,1)S(1)} %get-tuple-element.25) | copy-start | bytes 196612
  135.7 9.6 %copy-start.6 = (bf16[4,128,1,64]{3,1,0,2:T(8,128)(2,1)}, bf16[4,128,1,64]{3,1,0,2:T(8,128)(2,1)S(1)}, u32[]{:S(2)}) copy-start(bf16[4,128,1,64]{3,1,0,2:T(8,128)(2,1)S(1)} %get-tuple-element.26) | copy-start | bytes 196612
  200.4 204.8 %all-reduce.10.cloned.1.call-start = ((), (), s32[]{:S(2)}) async-start(), calls=%async_computation.2 | async-start | bytes 262144 | tf_op jit(solution)/shard_map/psum | solution.py:193
  308.8 2.7 copy-start.16
  311.6 133.9 %copy-start.11 = (s32[4,128,2]{1,2,0:T(2,128)S(1)}, s32[4,128,2]{1,2,0:T(2,128)}, u32[]{:S(2)}) copy-start(s32[4,128,2]{1,2,0:T(2,128)} %param.30) | copy-start | bytes 12292
  312.7 251.3 %reduce-scatter.5.cloned.1.call-start = ((), (), s32[]{:S(2)}) async-start(), calls=%async_computation.3 | async-start | bytes 2228224
  406.2 5.6 collective-permute-start
  411.8 5.6 collective-permute-start.1
  411.8 5.6 collective-permute-start.8
  417.4 5.6 collective-permute-start.2
  417.4 5.6 collective-permute-start.9
  423.0 5.6 collective-permute-start.3
  423.0 5.6 collective-permute-start.10
  428.6 5.6 collective-permute-start.4
  428.6 5.6 collective-permute-start.11
  434.2 5.6 collective-permute-start.5
  434.3 5.6 collective-permute-start.12
  439.8 5.6 collective-permute-start.6
  439.9 6.5 collective-permute-start.13
  445.5 5.6 collective-permute-start.7
  446.4 14.6 %collective-permute-start.14 = (bf16[4,128,128]{2,1,0:T(8,128)(2,1)S(1)}, bf16[4,128,128]{2,1,0:T(8,128)(2,1)S(1)}, u32[]{:S(2)}, u32[]{:S(2)}) collective-permute-start(bf16[4,128,128]{2,1,0:T(8,128)(2,1)S(1)} %collective-permute-done.13), channel_id=1, source_target_pairs={{16,0},{32,16},{48,32},{64,48},{80,64},{96,80},{112,96},{128,112},... | collective-permute-start | bytes 393224 | tf_op jit(solution)/shard_map/ppermute | solution.py:203
  472.5 6.7 %copy-start.1 = (f32[4,128,16,128]{1,3,2,0:T(8,128)S(1)}, f32[4,128,16,128]{1,3,2,0:T(8,128)}, u32[]{:S(2)}) copy-start(f32[4,128,16,128]{1,3,2,0:T(8,128)} %copy.143) | copy-start | bytes 12582916
  472.5 6.7 %copy-start.9 = (f32[2048]{0:T(1024)S(1)}, f32[2048]{0:T(1024)}, u32[]{:S(2)}) copy-start(f32[2048]{0:T(1024)} %param.22) | copy-start | bytes 24580
  479.2 0.8 copy-start.17
  480.0 0.9 copy-start.2
  490.0 4.1 copy-start.15
  504.7 0.7 copy-start.19
  504.7 61.0 %copy-start.5 = (bf16[4,128,1,64]{3,1,0,2:T(8,128)(2,1)S(1)}, bf16[4,128,1,64]{3,1,0,2:T(8,128)(2,1)}, u32[]{:S(2)}) copy-start(bf16[4,128,1,64]{3,1,0,2:T(8,128)(2,1)} %copy-done.4) | copy-start | bytes 196612
  504.7 61.0 %copy-start.7 = (bf16[4,128,1,64]{3,1,0,2:T(8,128)(2,1)S(1)}, bf16[4,128,1,64]{3,1,0,2:T(8,128)(2,1)}, u32[]{:S(2)}) copy-start(bf16[4,128,1,64]{3,1,0,2:T(8,128)(2,1)} %copy-done.6) | copy-start | bytes 196612
  504.8 152.8 %all-reduce.12.cloned.1.call-start = ((), (), s32[]{:S(2)}) async-start(), calls=%async_computation.4 | async-start | bytes 262144
Sparse Core Ops, SparseCore 0:
  13.3 119.8 all-reduce.13
  200.6 107.0 all-reduce.7
  312.8 92.4 all-reduce.9
  504.9 59.0 reduce-scatter.4
  567.0 90.4 all-reduce.11
